TPU v7x, 128 devices: a whole 4x4x4 slice. The times are simulated.
128 devices in a mesh: cfg: 2 (over core), row: 4 (over z), col: 16 (over y, x).
Axes of the slice: x: 4, y: 4, z: 4, core: 2. Of those that a mesh axis runs over, the one named last changes fastest.
Arguments:
- img_tokens: bfloat16 [2, 16, 1024, 3072], P('cfg', 'col', None, 'row'), may hold values from -6 to 6
- txt_tokens: bfloat16 [2, 16, 512, 3072], P('cfg', 'col', None, 'row'), may hold values from -6 to 6
- img_mod: bfloat16 [2, 16, 2, 3072], P('cfg', 'col', None, 'row'), may hold values from -3 to 3
- txt_mod: bfloat16 [2, 16, 2, 3072], P('cfg', 'col', None, 'row'), may hold values from -3 to 3
- img_gate: bfloat16 [2, 16, 3072], P('cfg', 'col', 'row'), may hold values from -16 to 16
- txt_len: int32 [2, 16], P('cfg', 'col'), may hold values from 128 to 512, as said below
- img_qkv_weight: bfloat16 [3072, 3, 3072], P('col', None, 'row'), may hold values from -0.109375 to 0.109375
- txt_kv_weight: bfloat16 [3072, 2, 3072], P('col', None, 'row'), may hold values from -0.109375 to 0.109375
- out_weight: bfloat16 [3072, 3072], P('row', 'col'), may hold values from -0.109375 to 0.109375
- final_weight: bfloat16 [3072, 64], P('row'), may hold values from -0.109375 to 0.109375
- latent: float32 [16, 1024, 64], P('col', ('cfg', 'row')), may hold values from -6 to 6
- sigmas: float32 [5], replicated, may hold values from 0 to 2, as said below
- step_index: int32 [1], replicated, may hold values from 0 to 3
- guidance: float32 [1], replicated, may hold values from 1.5 to 5
Outputs:
- img_out: bfloat16 [2, 16, 1024, 3072], P('cfg', 'col', None, 'row')
- latent_next: float32 [16, 1024, 64], P('col', ('cfg', 'row'))
Inputs may be any that keep to these rules, and one draw needn't show every extreme that they name: `txt_len`: in each half some prompt has all 512 text slots live and some other prompt exactly 128. `sigmas`: falls strictly along the table.
All inputs are finite; a program needn't handle non-finite values.
Results may differ from a plain program's by a relative error of at most 0.015.
Values may be sent and summed in bfloat16 or wider, within the bound.
No kernel may reach another device: no remote copies, remote signals or barrier semaphores. Data moves between devices by JAX's collectives and lax.ppermute only.
A program may use at most 128 MiB of HBM per device.

v0:
```python
import math
import jax
import jax.numpy as jnp
from jax import lax
from jax.sharding import PartitionSpec as P

HD = 128


def modulate(tokens, shift_scale):
    values = tokens.astype(jnp.float32)
    centre = values - jnp.mean(values, -1, keepdims=True)
    spread = jnp.mean(centre * centre, -1, keepdims=True)
    normed = centre * lax.rsqrt(spread + 1e-06)
    scaled = normed * (1.0 + shift_scale[..., 1:2, :].astype(jnp.float32))
    return (scaled + shift_scale[..., 0:1, :].astype(jnp.float32)).astype(jnp.bfloat16)


def rms_norm(values):
    return values * lax.rsqrt(jnp.mean(values * values, -1, keepdims=True) + 1e-06)


def add_rows(piece, ready):
    return jnp.dot(ready, piece.reshape(piece.shape[0], -1), preferred_element_type=jnp.float32)


def shards(
    img_tokens,
    txt_tokens,
    img_mod,
    txt_mod,
    img_gate,
    txt_len,
    img_qkv_weight,
    txt_kv_weight,
    out_weight,
    final_weight,
    latent,
    sigmas,
    step_index,
    guidance,
):
    img_whole, txt_whole, img_shift, txt_shift = (
        lax.all_gather(img_tokens, "row", axis=3, tiled=True),
        lax.all_gather(txt_tokens, "row", axis=3, tiled=True),
        lax.all_gather(img_mod, "row", axis=3, tiled=True),
        lax.all_gather(txt_mod, "row", axis=3, tiled=True),
    )
    prompts = img_tokens.shape[1]
    images = img_tokens.shape[2]
    text_slots = txt_tokens.shape[2]
    local_width = img_qkv_weight.shape[2]
    heads_here = local_width // HD
    img_ready = modulate(img_whole[0], img_shift[0]).reshape(prompts * images, -1)
    txt_ready = modulate(txt_whole[0], txt_shift[0]).reshape(prompts * text_slots, -1)
    img_proj = add_rows(lax.all_gather(img_qkv_weight, "col", axis=0, tiled=True), img_ready)
    txt_proj = add_rows(lax.all_gather(txt_kv_weight, "col", axis=0, tiled=True), txt_ready)
    img_proj = img_proj.reshape(prompts, images, 3, heads_here, HD)
    txt_proj = txt_proj.reshape(prompts, text_slots, 2, heads_here, HD)
    queries = rms_norm(img_proj[:, :, 0]).astype(jnp.bfloat16)
    key_rows = jnp.concatenate(
        [rms_norm(txt_proj[:, :, 0]), rms_norm(img_proj[:, :, 1])], 1
    ).astype(jnp.bfloat16)
    value_rows = jnp.concatenate([txt_proj[:, :, 1], img_proj[:, :, 2]], 1).astype(jnp.bfloat16)
    positions = jnp.arange(text_slots + images, dtype=jnp.int32)
    scores = jnp.einsum(
        "qhe,khe->hqk", queries[0], key_rows[0], preferred_element_type=jnp.float32
    ) / math.sqrt(HD)
    usable = (positions < txt_len[0, 0]) | (positions >= text_slots)
    weights = jnp.where(usable, jnp.exp(scores), 0.0)
    chances = (weights / jnp.sum(weights, -1, keepdims=True)).astype(jnp.bfloat16)
    mixed = jnp.einsum("hqk,khe->qhe", chances, value_rows[0], preferred_element_type=jnp.float32)
    outputs = mixed.reshape(images, local_width).astype(jnp.bfloat16)
    head_terms = jnp.dot(
        outputs,
        lax.all_gather(out_weight, "col", axis=1, tiled=True),
        preferred_element_type=jnp.float32,
    )
    projected = (
        lax.psum_scatter(head_terms.astype(jnp.bfloat16), "row", scatter_dimension=1, tiled=True)
        .astype(jnp.float32)
        .reshape(prompts, images, local_width)
    )
    gating = img_gate[0][:, None, :].astype(jnp.float32)
    img_out = (img_tokens[0].astype(jnp.float32) + gating * projected).astype(jnp.bfloat16)
    velocity = jnp.dot(
        img_out.reshape(prompts * images, local_width),
        final_weight,
        preferred_element_type=jnp.float32,
    )
    velocity = velocity.reshape(prompts, images, -1)
    strength = guidance[0]
    share = jnp.where(lax.axis_index("cfg") == 1, strength, 1.0 - strength)
    weighted = velocity * share
    halved = lax.psum_scatter(weighted.astype(jnp.bfloat16), "cfg", scatter_dimension=1, tiled=True)
    guided = lax.psum_scatter(halved, "row", scatter_dimension=1, tiled=True).astype(jnp.float32)
    position_now = step_index[0]
    step_size = sigmas[position_now + 1] - sigmas[position_now]
    return (img_out[None], latent + step_size * guided)


def solution(mesh):
    return jax.shard_map(
        shards,
        mesh=mesh,
        in_specs=(
            P("cfg", "col", None, "row"),
            P("cfg", "col", None, "row"),
            P("cfg", "col", None, "row"),
            P("cfg", "col", None, "row"),
            P("cfg", "col", "row"),
            P("cfg", "col"),
            P("col", None, "row"),
            P("col", None, "row"),
            P("row", "col"),
            P("row", None),
            P("col", ("cfg", "row"), None),
            P(),
            P(),
            P(),
        ),
        out_specs=(P("cfg", "col", None, "row"), P("col", ("cfg", "row"), None)),
        check_vma=False,
    )
```

profile of v0, /device:TPU:0, one launch (start us, length us, event | category | flops | bytes accessed | tf_op | source)
XLA Modules:
  0.0 494.2 jit_solution(1742859976843953743)
XLA Ops:
  7.2 0.0 copy-start
  7.2 0.0 all-gather.6.cloned.1.call-start
  7.2 0.7 all-gather.6.cloned.1.call-update
  7.9 0.0 all-gather.10.cloned.1.call-start
  8.0 0.7 all-gather.10.cloned.1.call-update
  8.7 0.0 all-gather.8.cloned.1.call-start
  8.7 0.7 all-gather.8.cloned.1.call-update
  9.4 0.0 all-gather.12.cloned.1.call-start
  9.4 0.5 all-gather.12.cloned.1.call-update
  10.0 0.0 all-gather.14.cloned.1.call-start
  10.0 0.5 all-gather.14.cloned.1.call-update
  10.6 0.0 reduce-scatter.6.cloned.1.call-start
  10.6 13.4 %all_gather.25 = bf16[1,1,2,3072]{3,2,1,0:T(2,128)(2,1)S(1)} all-gather(bf16[1,1,2,768]{3,2,1,0:T(2,128)(2,1)} %param.16), channel_id=1, replica_groups=mesh['cfg'=2,'row'=4,'col'=16] {'row'}, dimensions={3}, use_global_device_ids=true | all-gather | bytes 15360 | tf_op jit(solution)/shard_map/all_gather | solution.py:46
  24.0 12.4 %all_gather.22 = bf16[1,1,2,3072]{3,2,1,0:T(2,128)(2,1)S(1)} all-gather(bf16[1,1,2,768]{3,2,1,0:T(2,128)(2,1)} %param.17), channel_id=1, replica_groups=mesh['cfg'=2,'row'=4,'col'=16] {'row'}, dimensions={3}, use_global_device_ids=true | all-gather | bytes 15360 | tf_op jit(solution)/shard_map/all_gather | solution.py:47
  37.2 14.8 %all-gather.6.cloned.1.call-done = bf16[1,1,512,3072]{3,2,1,0:T(8,128)(2,1)} async-done(((bf16[1,1,512,768]{3,2,1,0:T(8,128)(2,1)}), bf16[1,1,512,3072]{3,2,1,0:T(8,128)(2,1)}) %all-gather.6.cloned.1.call-update) | async-done | bytes 3145744 | tf_op jit(solution)/shard_map/all_gather | solution.py:45
  52.0 0.0 copy-start.3
  52.0 2.5 convert_reduce_fusion.1
  54.5 0.3 copy-done.3
  54.8 1.0 fusion.15
  55.8 63.7 %all-gather.10.cloned.1.call-done = bf16[1,1,1024,3072]{3,2,1,0:T(8,128)(2,1)} async-done(((bf16[1,1,1024,768]{3,2,1,0:T(8,128)(2,1)}), bf16[1,1,1024,3072]{3,2,1,0:T(8,128)(2,1)}) %all-gather.10.cloned.1.call-update) | async-done | bytes 6291472 | tf_op jit(solution)/shard_map/all_gather | solution.py:44
  119.5 3.8 convert_reduce_fusion
  123.3 0.8 copy-done.1
  124.1 1.8 fusion.8
  125.9 71.7 %all-gather.8.cloned.1.call-done = bf16[3072,2,768]{2,1,0:T(2,128)(2,1)} async-done(((bf16[192,2,768]{2,1,0:T(2,128)(2,1)}), bf16[3072,2,768]{2,1,0:T(2,128)(2,1)}) %all-gather.8.cloned.1.call-update) | async-done | bytes 9437200 | tf_op jit(solution)/shard_map/all_gather | solution.py:57
  197.6 23.8 %copy.27 = bf16[3072,2,768]{0,2,1:T(8,128)(2,1)} copy(bf16[3072,2,768]{2,1,0:T(2,128)(2,1)} %all-gather.8.cloned.1.call-done) | data formatting | bytes 18874368 | tf_op jit(solution)/shard_map/reshape | solution.py:24
  221.4 8.5 %fusion.43 = f32[1,512,2,6,128]{4,1,3,2,0:T(8,128)S(1)} fusion(bf16[2,6,128,3072]{3,2,1,0:T(8,128)(2,1)} %bitcast.111, bf16[1,1,512,3072]{3,2,1,0:T(8,128)(2,1)S(1)} %copy-done.3, f32[3072]{0:T(1024)S(1)} %bitcast.121, f32[3072]{0:T(1024)S(1)} %bitcast.120, f32[512]{0:T(512)S(1)} %add_rsqrt_fusion.4, f32[512]{0:T(512)S(1)} %broadcast_multiply_fusion.1), kind=kOutput, calls=%fused_computation.54 | convolution fusion | flops 4841275392 | bytes 15757312 | tf_op jit(solution)/shard_map/dot_general | solution.py:24
  229.9 0.5 multiply_reduce_fusion.2
  230.4 1.0 fusion.55
  231.4 1.4 fusion.51
  232.7 64.3 %all-gather.12.cloned.1.call-done = bf16[3072,3,768]{2,0,1:T(8,128)(2,1)} async-done(((bf16[192,3,768]{2,0,1:T(8,128)(2,1)}), bf16[3072,3,768]{2,0,1:T(8,128)(2,1)}) %all-gather.12.cloned.1.call-update) | async-done | bytes 14155792 | tf_op jit(solution)/shard_map/all_gather | solution.py:56
  297.0 18.7 %copy.22 = bf16[3072,3,768]{0,2,1:T(8,128)(2,1)} copy(bf16[3072,3,768]{2,0,1:T(8,128)(2,1)} %all-gather.12.cloned.1.call-done) | data formatting | bytes 28311552 | tf_op jit(solution)/shard_map/all_gather | solution.py:56
  315.7 21.6 %fusion.23 = f32[1,1024,3,6,128]{4,1,3,2,0:T(8,128)S(1)} fusion(bf16[3,6,128,3072]{3,2,1,0:T(8,128)(2,1)} %bitcast.110, bf16[1,1,1024,3072]{3,2,1,0:T(8,128)(2,1)} %all-gather.10.cloned.1.call-done, f32[3072]{0:T(1024)S(1)} %bitcast.119, f32[3072]{0:T(1024)S(1)} %bitcast.118, f32[1024]{0:T(1024)S(1)} %add_rsqrt_fusion.3, f32[1024]{0:T(1024)S(1)} %broadcast_multiply_fusion), kind=kOutput, calls=%fused_computation.31 | convolution fusion | flops 14514388992 | bytes 29917184 | tf_op jit(solution)/shard_map/dot_general | solution.py:24
  337.3 0.0 copy-start.2
  337.4 1.7 multiply_reduce_fusion.1
  339.1 1.0 fusion.30
  340.1 0.9 copy-done.2
  340.9 0.2 fusion.50
  341.2 18.4 %fusion = (f32[6,1024]{1,0:T(8,128)S(1)}, f32[6,1024,1536]{2,1,0:T(8,128)}) fusion(pred[1536]{0:T(1024)(128)(4,1)S(1)} %fusion.60, bf16[1024,6,128]{2,0,1:T(8,128)(2,1)S(1)} %fusion.30, bf16[512,6,128]{2,0,1:T(8,128)(2,1)} %fusion.51, f32[1,1024,3,6,128]{4,1,3,2,0:T(8,128)} %copy-done.2, f32[1024,6]{0,1:T(8,128)S(1)} %get-tuple-element.9), kind=kOutput, calls=%fused_computation.2 | convolution fusion | flops 2450515968 | bytes 43304448 | tf_op jit(solution)/shard_map/qhe,khe->hqk/dot_general | solution.py:66
  359.5 15.2 %fusion.46 = bf16[6,128,1024]{2,1,0:T(8,128)(2,1)S(1)} fusion(f32[6,1024,1536]{2,1,0:T(8,128)} %get-tuple-element.7, f32[6,1024]{1,0:T(8,128)S(1)} %get-tuple-element.6, pred[1536]{0:T(1024)(128)(4,1)S(1)} %fusion.60, bf16[1024,6,128]{2,0,1:T(8,128)(2,1)S(1)} %fusion.50, bf16[512,6,128]{2,0,1:T(8,128)(2,1)} %fusion.55), kind=kOutput, calls=%fused_computation.55 | convolution fusion | flops 2459172864 | bytes 41707008 | tf_op jit(solution)/shard_map/hqk,khe->qhe/dot_general | solution.py:72
  374.8 0.0 all-gather.14.cloned.1.call-done
  374.8 9.4 %convolution_convert_fusion = bf16[1024,3072]{1,0:T(8,128)(2,1)} fusion(bf16[1024,768]{0,1:T(8,128)(2,1)S(1)} %bitcast.122, bf16[768,3072]{0,1:T(8,128)(2,1)} %all-gather.14.cloned.1.call-done), kind=kOutput, calls=%fused_computation.30 | convolution fusion | flops 4834983936 | bytes 12582912 | tf_op jit(solution)/shard_map/dot_general | solution.py:74
  384.2 0.0 reduce-scatter.6.cloned.1.call-update
  384.2 0.0 reduce-scatter.8.cloned.1.call-start
  385.0 0.0 copy-done.7
  385.1 0.0 copy-start.6
  385.1 63.3 %reduce-scatter.6.cloned.1.call-done = bf16[1024,768]{1,0:T(8,128)(2,1)} async-done(((bf16[1024,3072]{1,0:T(8,128)(2,1)}), bf16[1024,768]{1,0:T(8,128)(2,1)}) %reduce-scatter.6.cloned.1.call-update) | async-done | bytes 1572880 | tf_op jit(solution)/shard_map/reduce_scatter | solution.py:80
  448.4 0.0 copy-done
  448.4 0.0 copy-done.4
  448.4 2.9 fusion.54
  451.2 0.0 reduce-scatter.8.cloned.1.call-update
  451.2 0.0 reduce-scatter.10.cloned.1.call-start
  451.9 0.0 copy-done.8
  452.0 0.6 fusion.65
  453.8 7.3 %reduce-scatter.8.cloned.1.call-done = bf16[1,512,64]{1,2,0:T(8,128)(2,1)} async-done(((bf16[1,1024,64]{1,2,0:T(8,128)(2,1)}), bf16[1,512,64]{1,2,0:T(8,128)(2,1)}) %reduce-scatter.8.cloned.1.call-update) | async-done | bytes 65552 | tf_op jit(solution)/shard_map/reduce_scatter | solution.py:95
  461.1 1.0 copy.28
  462.1 0.7 copy.32
  462.7 0.0 reduce-scatter.10.cloned.1.call-update
  462.7 0.0 copy-done.5
  462.8 1.6 fusion.57
  464.4 21.4 %reduce-scatter.10.cloned.1.call-done = bf16[128,64]{1,0:T(8,128)(2,1)} async-done(((bf16[512,64]{1,0:T(8,128)(2,1)}), bf16[128,64]{1,0:T(8,128)(2,1)}) %reduce-scatter.10.cloned.1.call-update) | async-done | bytes 16400
  485.8 0.8 reshape_bitcast_fusion
  486.6 0.1 copy.29
  486.7 0.0 copy-done.6
  486.7 0.6 multiply_add_fusion
  (17 shorter events, 0.1 us)
Async XLA Ops:
  7.2 441.2 %copy-start = (bf16[768,64]{0,1:T(8,128)(2,1)S(1)}, bf16[768,64]{0,1:T(8,128)(2,1)}, u32[]{:S(2)}) copy-start(bf16[768,64]{0,1:T(8,128)(2,1)} %param.23) | copy-start | bytes 294916
  7.2 44.8 %all-gather.6.cloned.1.call-start = ((), (), s32[]{:S(2)}) async-start(), calls=%async_computation.3 | async-start | bytes 3932160 | tf_op jit(solution)/shard_map/all_gather | solution.py:45
  7.9 111.6 %all-gather.10.cloned.1.call-start = ((), (), s32[]{:S(2)}) async-start(), calls=%async_computation.5 | async-start | bytes 7864320 | tf_op jit(solution)/shard_map/all_gather | solution.py:44
  8.7 188.9 %all-gather.8.cloned.1.call-start = ((), (), s32[]{:S(2)}) async-start(), calls=%async_computation.4 | async-start | bytes 10027008 | tf_op jit(solution)/shard_map/all_gather | solution.py:57
  9.4 287.6 %all-gather.12.cloned.1.call-start = ((), (), s32[]{:S(2)}) async-start(), calls=%async_computation.6 | async-start | bytes 15040512 | tf_op jit(solution)/shard_map/all_gather | solution.py:56
  10.0 364.8 %all-gather.14.cloned.1.call-start = ((), (), s32[]{:S(2)}) async-start(), calls=%async_computation.7 | async-start | bytes 5013504 | tf_op jit(solution)/shard_map/all_gather | solution.py:76
  10.6 437.8 %reduce-scatter.6.cloned.1.call-start = ((), (), s32[]{:S(2)}) async-start(), calls=%async_computation.8 | async-start | bytes 7864320 | tf_op jit(solution)/shard_map/reduce_scatter | solution.py:80
  52.0 2.8 copy-start.3
  119.5 4.6 copy-start.1
  337.3 3.6 copy-start.2
  384.2 0.8 copy-start.7
  384.2 64.1 %copy-start.4 = (bf16[1,1,1024,768]{3,2,1,0:T(8,128)(2,1)S(1)}, bf16[1,1,1024,768]{3,2,1,0:T(8,128)(2,1)}, u32[]{:S(2)}) copy-start(bf16[1,1,1024,768]{3,2,1,0:T(8,128)(2,1)} %param.14) | copy-start | bytes 4718596
  384.2 67.7 %copy-start.8 = (f32[5]{0:T(128)S(1)}, f32[5]{0:T(128)}, u32[]{:S(2)}) copy-start(f32[5]{0:T(128)} %param.25) | copy-start | bytes 64
  384.2 76.8 %reduce-scatter.8.cloned.1.call-start = ((), (), s32[]{:S(2)}) async-start(), calls=%async_computation.9 | async-start | bytes 196608 | tf_op jit(solution)/shard_map/reduce_scatter | solution.py:95
  385.1 101.6 %copy-start.6 = (f32[1,128,64]{1,2,0:T(8,128)S(1)}, f32[1,128,64]{1,2,0:T(8,128)}, u32[]{:S(2)}) copy-start(f32[1,128,64]{1,2,0:T(8,128)} %param.24) | copy-start | bytes 98308
  448.4 14.4 %copy-start.5 = (bf16[1024,768]{1,0:T(8,128)(2,1)S(1)}, bf16[1024,768]{1,0:T(8,128)(2,1)}, u32[]{:S(2)}) copy-start(bf16[1024,768]{1,0:T(8,128)(2,1)} %reduce-scatter.6.cloned.1.call-done) | copy-start | bytes 4718596
  451.2 34.6 %reduce-scatter.10.cloned.1.call-start = ((), (), s32[]{:S(2)}) async-start(), calls=%async_computation.10 | async-start | bytes 163840
Sparse Core Ops, SparseCore 0:
  9.6 42.2 all-gather.5
  53.6 65.8 all-gather.9
  121.7 75.8 all-gather.7
  199.6 97.3 all-gather.11
  299.0 53.3 all-gather.13
  384.4 63.9 reduce-scatter.5
  451.4 9.6 reduce-scatter.7
  463.4 22.3 reduce-scatter.9
where the time goes:
time: 496 us; the launch traced here: 494 us
  waiting for transfers between devices  310 us (62%)
  matrix products  76 us (15%)
  local copies, waits for them, and re-layouts  48.8 us (10%)
  blocking collectives  25.8 us (5%)
  between operations  17.6 us (4%)
  other arithmetic  15.9 us (3%)
    all_gather x1, waiting for transfers between devices, shards(): lax.all_gather(txt_kv_weight, 'col', axis=0, tiled=True)  71.7 us
    all_gather x1, waiting for transfers between devices, shards(): lax.all_gather(img_qkv_weight, 'col', axis=0, tiled=True)  64.3 us
    all_gather x1, waiting for transfers between devices, shards(): lax.all_gather(img_tokens, 'row', axis=3, tiled=True)  63.7 us
    reduce_scatter x1, waiting for transfers between devices, shards(): lax.psum_scatter(head_terms.astype(jnp.bfloat16), 'row', scatter_dimensio...  63.3 us
    dot_general x2, matrix products, add_rows(): jnp.dot(ready, piece.reshape(piece.shape[0], -1), preferred_element_type=...  30.1 us
    unnamed x9, waiting for transfers between devices  24.6 us
    reshape x1, local copies, waits for them, and re-layouts, add_rows(): piece.reshape(piece.shape[0], -1)  23.8 us
    all_gather x1, local copies, waits for them, and re-layouts, shards(): lax.all_gather(img_qkv_weight, 'col', axis=0, tiled=True)  18.7 us
  transfers between devices with their start and end apart: 8, of which 7 were waited for; matrix products, arithmetic and copies ran while one was open for 25% of the time, Pallas kernels for 0%

commit v1 on v0

--- a/solution.py
+++ b/solution.py
@@ -43,7 +43,9 @@
     img_whole, txt_whole, img_shift, txt_shift = (
         lax.all_gather(img_tokens, "row", axis=3, tiled=True),
         lax.all_gather(txt_tokens, "row", axis=3, tiled=True),
-        lax.all_gather(img_mod, "row", axis=3, tiled=True),
+        jnp.concatenate(
+            lax.all_to_all(jnp.stack([img_mod] * lax.axis_size("row")), "row", 0, 0), axis=3
+        ),
         lax.all_gather(txt_mod, "row", axis=3, tiled=True),
     )
     prompts = img_tokens.shape[1]

time: 496 us -> 496 us (level)
  blocking collectives: 25.8 us -> 13 us
  waiting for transfers between devices: 310 us -> 316 us
  starting transfers between devices: 0.31 us -> 5.69 us
    all_gather x1 -> x0, blocking collectives: 13.4 us -> none  [shards(): lax.all_gather(img_mod, 'row', axis=3, tiled=True)]
    all_gather x1, waiting for transfers between devices: 14.8 us -> 20.8 us  [shards(): lax.all_gather(txt_tokens, 'row', axis=3, tiled=True)]
    all_to_all x0 -> x1, starting transfers between devices: none -> 5.42 us  [shards(): lax.all_to_all(jnp.stack([img_mod] * lax.axis_size('row')), 'row', 0, 0)]
  transfers between devices with their start and end apart: 8 -> 9, of which waited for: 7 -> 7; matrix products, arithmetic and copies ran while one was open for 25% -> 25% of each run, Pallas kernels for 0% -> 0%
where the time goes in v1:
time: 496 us; the launch traced here: 494 us
  waiting for transfers between devices  316 us (64%)
  matrix products  76 us (15%)
  local copies, waits for them, and re-layouts  50.2 us (10%)
  between operations  17.6 us (4%)
  other arithmetic  15.9 us (3%)
  blocking collectives  13 us (3%)
  starting transfers between devices  5.69 us (1%)
    all_gather x1, waiting for transfers between devices, shards(): lax.all_gather(txt_kv_weight, 'col', axis=0, tiled=True)  71.7 us
    all_gather x1, waiting for transfers between devices, shards(): lax.all_gather(img_qkv_weight, 'col', axis=0, tiled=True)  64.2 us
    all_gather x1, waiting for transfers between devices, shards(): lax.all_gather(img_tokens, 'row', axis=3, tiled=True)  63.7 us
    reduce_scatter x1, waiting for transfers between devices, shards(): lax.psum_scatter(head_terms.astype(jnp.bfloat16), 'row', scatter_dimensio...  63.3 us
    dot_general x2, matrix products, add_rows(): jnp.dot(ready, piece.reshape(piece.shape[0], -1), preferred_element_type=...  30.1 us
    unnamed x9, waiting for transfers between devices  24.7 us
    reshape x1, local copies, waits for them, and re-layouts, add_rows(): piece.reshape(piece.shape[0], -1)  23.9 us
    all_gather x1, waiting for transfers between devices, shards(): lax.all_gather(txt_tokens, 'row', axis=3, tiled=True)  20.8 us
  transfers between devices with their start and end apart: 9, of which 7 were waited for; matrix products, arithmetic and copies ran while one was open for 25% of the time, Pallas kernels for 0%

profile of v1, /device:TPU:0, one launch (start us, length us, event | category | flops | bytes accessed | tf_op | source)
XLA Modules:
  0.0 494.2 jit_solution(11897025679552153372)
XLA Ops:
  7.2 0.0 copy-start
  7.2 0.0 all-gather.6.cloned.1.call-start
  7.2 0.7 all-gather.6.cloned.1.call-update
  7.9 0.0 all-gather.10.cloned.1.call-start
  8.0 0.7 all-gather.10.cloned.1.call-update
  8.7 0.0 all-gather.8.cloned.1.call-start
  8.7 0.7 all-gather.8.cloned.1.call-update
  9.4 0.0 all-gather.12.cloned.1.call-start
  9.4 0.5 all-gather.12.cloned.1.call-update
  10.0 1.3 stack.2
  11.3 5.4 %all-to-all-start = ((bf16[4,1,1,2,768]{4,3,2,1,0:T(2,128)(2,1)}), bf16[4,1,1,2,768]{4,3,2,1,0:T(2,128)(2,1)S(1)}, u32[]{:S(2)}, u32[]{:S(2)}) async-start(bf16[4,1,1,2,768]{4,3,2,1,0:T(2,128)(2,1)} %stack.2), calls=%async_computation | async-start | bytes 24576 | tf_op jit(solution)/shard_map/all_to_all | solution.py:47
  16.7 0.0 all-gather.14.cloned.1.call-start
  16.7 0.6 all-gather.14.cloned.1.call-update
  17.3 0.0 reduce-scatter.6.cloned.1.call-start
  17.3 13.0 %all_gather.19 = bf16[1,1,2,3072]{3,2,1,0:T(2,128)(2,1)S(1)} all-gather(bf16[1,1,2,768]{3,2,1,0:T(2,128)(2,1)} %param.17), channel_id=1, replica_groups=mesh['cfg'=2,'row'=4,'col'=16] {'row'}, dimensions={3}, use_global_device_ids=true | all-gather | bytes 15360 | tf_op jit(solution)/shard_map/all_gather | solution.py:49
  31.1 0.0 all-to-all-done
  31.1 20.8 %all-gather.6.cloned.1.call-done = bf16[1,1,512,3072]{3,2,1,0:T(8,128)(2,1)} async-done(((bf16[1,1,512,768]{3,2,1,0:T(8,128)(2,1)}), bf16[1,1,512,3072]{3,2,1,0:T(8,128)(2,1)}) %all-gather.6.cloned.1.call-update) | async-done | bytes 3145744 | tf_op jit(solution)/shard_map/all_gather | solution.py:45
  51.9 2.5 convert_reduce_fusion.1
  54.5 0.3 copy-done.3
  54.8 1.0 fusion.15
  55.7 63.7 %all-gather.10.cloned.1.call-done = bf16[1,1,1024,3072]{3,2,1,0:T(8,128)(2,1)} async-done(((bf16[1,1,1024,768]{3,2,1,0:T(8,128)(2,1)}), bf16[1,1,1024,3072]{3,2,1,0:T(8,128)(2,1)}) %all-gather.10.cloned.1.call-update) | async-done | bytes 6291472 | tf_op jit(solution)/shard_map/all_gather | solution.py:44
  119.5 3.8 convert_reduce_fusion
  123.3 0.8 copy-done.1
  124.1 1.8 fusion.8
  125.9 71.7 %all-gather.8.cloned.1.call-done = bf16[3072,2,768]{2,1,0:T(2,128)(2,1)} async-done(((bf16[192,2,768]{2,1,0:T(2,128)(2,1)}), bf16[3072,2,768]{2,1,0:T(2,128)(2,1)}) %all-gather.8.cloned.1.call-update) | async-done | bytes 9437200 | tf_op jit(solution)/shard_map/all_gather | solution.py:59
  197.6 23.9 %copy.27 = bf16[3072,2,768]{0,2,1:T(8,128)(2,1)} copy(bf16[3072,2,768]{2,1,0:T(2,128)(2,1)} %all-gather.8.cloned.1.call-done) | data formatting | bytes 18874368 | tf_op jit(solution)/shard_map/reshape | solution.py:24
  221.4 8.5 %fusion.43 = f32[1,512,2,6,128]{4,1,3,2,0:T(8,128)S(1)} fusion(bf16[2,6,128,3072]{3,2,1,0:T(8,128)(2,1)} %bitcast.114, bf16[1,1,512,3072]{3,2,1,0:T(8,128)(2,1)S(1)} %copy-done.3, f32[3072]{0:T(1024)S(1)} %bitcast.124, f32[3072]{0:T(1024)S(1)} %bitcast.123, f32[512]{0:T(512)S(1)} %add_rsqrt_fusion.4, f32[512]{0:T(512)S(1)} %broadcast_multiply_fusion.1), kind=kOutput, calls=%fused_computation.54 | convolution fusion | flops 4841275392 | bytes 15757312 | tf_op jit(solution)/shard_map/dot_general | solution.py:24
  229.9 0.5 multiply_reduce_fusion.2
  230.4 1.0 fusion.55
  231.4 1.4 fusion.51
  232.8 64.2 %all-gather.12.cloned.1.call-done = bf16[3072,3,768]{2,0,1:T(8,128)(2,1)} async-done(((bf16[192,3,768]{2,0,1:T(8,128)(2,1)}), bf16[3072,3,768]{2,0,1:T(8,128)(2,1)}) %all-gather.12.cloned.1.call-update) | async-done | bytes 14155792 | tf_op jit(solution)/shard_map/all_gather | solution.py:58
  297.0 18.7 %copy.22 = bf16[3072,3,768]{0,2,1:T(8,128)(2,1)} copy(bf16[3072,3,768]{2,0,1:T(8,128)(2,1)} %all-gather.12.cloned.1.call-done) | data formatting | bytes 28311552 | tf_op jit(solution)/shard_map/all_gather | solution.py:58
  315.7 21.6 %fusion.23 = f32[1,1024,3,6,128]{4,1,3,2,0:T(8,128)S(1)} fusion(bf16[3,6,128,3072]{3,2,1,0:T(8,128)(2,1)} %bitcast.113, bf16[1,1,1024,3072]{3,2,1,0:T(8,128)(2,1)} %all-gather.10.cloned.1.call-done, f32[3072]{0:T(1024)S(1)} %bitcast.122, f32[3072]{0:T(1024)S(1)} %bitcast.121, f32[1024]{0:T(1024)S(1)} %add_rsqrt_fusion.3, f32[1024]{0:T(1024)S(1)} %broadcast_multiply_fusion), kind=kOutput, calls=%fused_computation.31 | convolution fusion | flops 14514388992 | bytes 29917184 | tf_op jit(solution)/shard_map/dot_general | solution.py:24
  337.3 0.0 copy-start.2
  337.3 1.7 multiply_reduce_fusion.1
  339.0 1.0 fusion.30
  340.0 0.9 copy-done.2
  340.9 0.2 fusion.50
  341.1 18.4 %fusion = (f32[6,1024]{1,0:T(8,128)S(1)}, f32[6,1024,1536]{2,1,0:T(8,128)}) fusion(pred[1536]{0:T(1024)(128)(4,1)S(1)} %fusion.60, bf16[1024,6,128]{2,0,1:T(8,128)(2,1)S(1)} %fusion.30, bf16[512,6,128]{2,0,1:T(8,128)(2,1)} %fusion.51, f32[1,1024,3,6,128]{4,1,3,2,0:T(8,128)} %copy-done.2, f32[1024,6]{0,1:T(8,128)S(1)} %get-tuple-element.9), kind=kOutput, calls=%fused_computation.2 | convolution fusion | flops 2450515968 | bytes 43304448 | tf_op jit(solution)/shard_map/qhe,khe->hqk/dot_general | solution.py:68
  359.5 15.2 %fusion.46 = bf16[6,128,1024]{2,1,0:T(8,128)(2,1)S(1)} fusion(f32[6,1024,1536]{2,1,0:T(8,128)} %get-tuple-element.7, f32[6,1024]{1,0:T(8,128)S(1)} %get-tuple-element.6, pred[1536]{0:T(1024)(128)(4,1)S(1)} %fusion.60, bf16[1024,6,128]{2,0,1:T(8,128)(2,1)S(1)} %fusion.50, bf16[512,6,128]{2,0,1:T(8,128)(2,1)} %fusion.55), kind=kOutput, calls=%fused_computation.55 | convolution fusion | flops 2459172864 | bytes 41707008 | tf_op jit(solution)/shard_map/hqk,khe->qhe/dot_general | solution.py:74
  374.8 0.0 all-gather.14.cloned.1.call-done
  374.8 9.4 %convolution_convert_fusion = bf16[1024,3072]{1,0:T(8,128)(2,1)} fusion(bf16[1024,768]{0,1:T(8,128)(2,1)S(1)} %bitcast.126, bf16[768,3072]{0,1:T(8,128)(2,1)} %all-gather.14.cloned.1.call-done), kind=kOutput, calls=%fused_computation.30 | convolution fusion | flops 4834983936 | bytes 12582912 | tf_op jit(solution)/shard_map/dot_general | solution.py:76
  384.2 0.0 reduce-scatter.6.cloned.1.call-update
  384.2 0.0 reduce-scatter.8.cloned.1.call-start
  385.0 0.0 copy-done.7
  385.0 0.0 copy-start.6
  385.1 63.3 %reduce-scatter.6.cloned.1.call-done = bf16[1024,768]{1,0:T(8,128)(2,1)} async-done(((bf16[1024,3072]{1,0:T(8,128)(2,1)}), bf16[1024,768]{1,0:T(8,128)(2,1)}) %reduce-scatter.6.cloned.1.call-update) | async-done | bytes 1572880 | tf_op jit(solution)/shard_map/reduce_scatter | solution.py:82
  448.3 0.0 copy-done
  448.3 0.0 copy-done.4
  448.3 2.8 fusion.54
  451.2 0.0 reduce-scatter.8.cloned.1.call-update
  451.2 0.0 reduce-scatter.10.cloned.1.call-start
  451.9 0.0 copy-done.8
  451.9 0.6 fusion.65
  453.7 7.3 %reduce-scatter.8.cloned.1.call-done = bf16[1,512,64]{1,2,0:T(8,128)(2,1)} async-done(((bf16[1,1024,64]{1,2,0:T(8,128)(2,1)}), bf16[1,512,64]{1,2,0:T(8,128)(2,1)}) %reduce-scatter.8.cloned.1.call-update) | async-done | bytes 65552 | tf_op jit(solution)/shard_map/reduce_scatter | solution.py:97
  461.0 1.0 copy.28
  462.0 0.7 copy.32
  462.7 0.0 reduce-scatter.10.cloned.1.call-update
  462.7 1.6 fusion.57
  464.3 21.5 %reduce-scatter.10.cloned.1.call-done = bf16[128,64]{1,0:T(8,128)(2,1)} async-done(((bf16[512,64]{1,0:T(8,128)(2,1)}), bf16[128,64]{1,0:T(8,128)(2,1)}) %reduce-scatter.10.cloned.1.call-update) | async-done | bytes 16400
  485.8 0.8 reshape_bitcast_fusion
  486.6 0.1 copy.29
  486.7 0.0 copy-done.6
  486.7 0.6 multiply_add_fusion
  (19 shorter events, 0.1 us)
Async XLA Ops:
  7.2 441.2 %copy-start = (bf16[768,64]{0,1:T(8,128)(2,1)S(1)}, bf16[768,64]{0,1:T(8,128)(2,1)}, u32[]{:S(2)}) copy-start(bf16[768,64]{0,1:T(8,128)(2,1)} %param.23) | copy-start | bytes 294916
  7.2 44.8 %all-gather.6.cloned.1.call-start = ((), (), s32[]{:S(2)}) async-start(), calls=%async_computation.4 | async-start | bytes 3932160 | tf_op jit(solution)/shard_map/all_gather | solution.py:45
  7.9 111.6 %all-gather.10.cloned.1.call-start = ((), (), s32[]{:S(2)}) async-start(), calls=%async_computation.6 | async-start | bytes 7864320 | tf_op jit(solution)/shard_map/all_gather | solution.py:44
  8.7 188.9 %all-gather.8.cloned.1.call-start = ((), (), s32[]{:S(2)}) async-start(), calls=%async_computation.5 | async-start | bytes 10027008 | tf_op jit(solution)/shard_map/all_gather | solution.py:59
  9.4 287.6 %all-gather.12.cloned.1.call-start = ((), (), s32[]{:S(2)}) async-start(), calls=%async_computation.7 | async-start | bytes 15040512 | tf_op jit(solution)/shard_map/all_gather | solution.py:58
  11.3 19.8 %all-to-all-start = ((bf16[4,1,1,2,768]{4,3,2,1,0:T(2,128)(2,1)}), bf16[4,1,1,2,768]{4,3,2,1,0:T(2,128)(2,1)S(1)}, u32[]{:S(2)}, u32[]{:S(2)}) async-start(bf16[4,1,1,2,768]{4,3,2,1,0:T(2,128)(2,1)} %stack.2), calls=%async_computation | async-start | bytes 24576 | tf_op jit(solution)/shard_map/all_to_all | solution.py:47
  16.7 358.1 %all-gather.14.cloned.1.call-start = ((), (), s32[]{:S(2)}) async-start(), calls=%async_computation.8 | async-start | bytes 5013504 | tf_op jit(solution)/shard_map/all_gather | solution.py:78
  17.3 431.1 %reduce-scatter.6.cloned.1.call-start = ((), (), s32[]{:S(2)}) async-start(), calls=%async_computation.9 | async-start | bytes 7864320 | tf_op jit(solution)/shard_map/reduce_scatter | solution.py:82
  51.9 2.8 copy-start.3
  119.5 4.6 copy-start.1
  337.3 3.6 copy-start.2
  384.2 0.8 copy-start.7
  384.2 64.1 %copy-start.4 = (bf16[1,1,1024,768]{3,2,1,0:T(8,128)(2,1)S(1)}, bf16[1,1,1024,768]{3,2,1,0:T(8,128)(2,1)}, u32[]{:S(2)}) copy-start(bf16[1,1,1024,768]{3,2,1,0:T(8,128)(2,1)} %param.14) | copy-start | bytes 4718596
  384.2 67.7 %copy-start.8 = (f32[5]{0:T(128)S(1)}, f32[5]{0:T(128)}, u32[]{:S(2)}) copy-start(f32[5]{0:T(128)} %param.25) | copy-start | bytes 64
  384.2 76.8 %reduce-scatter.8.cloned.1.call-start = ((), (), s32[]{:S(2)}) async-start(), calls=%async_computation.10 | async-start | bytes 196608 | tf_op jit(solution)/shard_map/reduce_scatter | solution.py:97
  385.0 101.6 %copy-start.6 = (f32[1,128,64]{1,2,0:T(8,128)S(1)}, f32[1,128,64]{1,2,0:T(8,128)}, u32[]{:S(2)}) copy-start(f32[1,128,64]{1,2,0:T(8,128)} %param.24) | copy-start | bytes 98308
  448.3 14.4 %copy-start.5 = (bf16[1024,768]{1,0:T(8,128)(2,1)S(1)}, bf16[1024,768]{1,0:T(8,128)(2,1)}, u32[]{:S(2)}) copy-start(bf16[1024,768]{1,0:T(8,128)(2,1)} %reduce-scatter.6.cloned.1.call-done) | copy-start | bytes 4718596
  451.2 34.6 %reduce-scatter.10.cloned.1.call-start = ((), (), s32[]{:S(2)}) async-start(), calls=%async_computation.11 | async-start | bytes 163840
Sparse Core Ops, SparseCore 0:
  9.6 42.2 all-gather.5
  53.6 65.8 all-gather.9
  121.6 75.8 all-gather.7
  199.6 97.3 all-gather.11
  299.0 53.3 all-gather.13
  384.3 63.9 reduce-scatter.5
  451.3 9.6 reduce-scatter.7
  463.4 22.3 reduce-scatter.9
